TPU v7x, 256 devices: a whole 4x4x8 slice. The times are simulated.
256 devices in a mesh: seq: 32 (over y, z_hi, core), head: 8 (over z_lo, x).
Axes of the slice: x: 4, y: 4, z: 8 (z_hi: 4, z_lo: 2; z = z_hi * 2 + z_lo), core: 2. Of those that a mesh axis runs over, the one named last changes fastest.
Arguments:
- xin: bfloat16 [16384, 8192], P('seq', 'head'), may hold values from -6 to 6
- gate_z: bfloat16 [16384, 8192], P('seq', 'head'), may hold values from -6 to 6
- b_proj: bfloat16 [16384, 8, 256], P('seq', 'head'), may hold values from -0.375 to 0.375
- c_proj: bfloat16 [16384, 8, 256], P('seq', 'head'), may hold values from -0.375 to 0.375
- log_retain: float32 [16384, 128], P('seq', 'head'), may hold values from -2 to 0, as said below
- skip_d: float32 [128], P('head'), may hold values from 0.5 to 2
- norm_gain: float32 [8192], P('head'), may hold values from 0.5 to 1.5
- w_out: bfloat16 [8192, 4096], P('head', 'seq'), may hold values from -0.0625 to 0.0625
- residual: bfloat16 [16384, 4096], P(('seq', 'head')), may hold values from -24 to 24
- refusal: float32 [4096], replicated, may hold values from -6 to 6
- stream_gain: float32 [4096], replicated, may hold values from 0.5 to 1.5
- w_in: bfloat16 [4096, 8192], P('seq', 'head'), may hold values from -0.09375 to 0.09375
Outputs:
- stream: bfloat16 [16384, 4096], P(('seq', 'head'))
- next_x: bfloat16 [16384, 8192], P('seq', 'head')
Inputs may be any that keep to these rules, and one draw needn't show every extreme that they name: `log_retain`: every entry is negative.
All inputs are finite; a program needn't handle non-finite values.
Results may differ from a plain program's by a relative error of at most 0.02.
Values may be sent and summed in bfloat16 or wider, within the bound.
No kernel may reach another device: no remote copies, remote signals or barrier semaphores. Data moves between devices by JAX's collectives and lax.ppermute only.
A program may use at most 192 MiB of HBM per device.

v0:
```python
import jax
import jax.numpy as jnp
from jax import lax
from jax.sharding import PartitionSpec as P

SPAN = 256


def prefix(array, axis, combine, identity):
    devices, place = (lax.axis_size(axis), lax.axis_index(axis))
    everything = jax.tree.map(
        lambda part, kind: lax.all_gather(part.astype(kind), axis),
        array,
        (jnp.bfloat16, jnp.bfloat16),
    )
    start = jax.tree.map(
        lambda part, zero: jnp.broadcast_to(jnp.asarray(zero, part.dtype), part.shape),
        array,
        identity,
    )

    def turn(k, before):
        reached = k < place
        new = combine(
            before, jax.tree.map(lambda part, own: part[k].astype(own.dtype), everything, array)
        )
        return jax.tree.map(lambda a, b: jnp.where(reached, a, b), new, before)

    return lax.fori_loop(0, devices, turn, start)


def carry_combine(earlier, later):
    decay_early, state_early = earlier
    decay_later, state_later = later
    return (
        decay_early + decay_later,
        jnp.exp(decay_later)[:, None, None] * state_early + state_later,
    )


def body(
    xin,
    gate_z,
    b_proj,
    c_proj,
    log_retain,
    skip_d,
    norm_gain,
    w_out,
    residual,
    refusal,
    stream_gain,
    w_in,
):
    seq_rows, channels = xin.shape
    head_count = log_retain.shape[1]
    head_width = channels // head_count
    group_count = b_proj.shape[1]
    state_width = b_proj.shape[2]
    per_group = head_count // group_count
    block_count = seq_rows // SPAN
    inputs = xin.reshape(block_count, SPAN, head_count, head_width)
    b_grouped = b_proj.reshape(block_count, SPAN, group_count, state_width)
    c_grouped = c_proj.reshape(block_count, SPAN, group_count, state_width)
    scores = jnp.einsum("klgn,ksgn->kgls", c_grouped, b_grouped, preferred_element_type=jnp.float32)
    scores = jnp.repeat(scores, per_group, axis=1)
    cum = jnp.cumsum(log_retain.reshape(block_count, SPAN, head_count), axis=1)
    cum_heads = jnp.transpose(cum, (0, 2, 1))
    later_pos = lax.broadcasted_iota(jnp.int32, (SPAN, SPAN), 0)
    earlier_pos = lax.broadcasted_iota(jnp.int32, (SPAN, SPAN), 1)
    causal = later_pos >= earlier_pos
    gap = cum_heads[:, :, :, None] - cum_heads[:, :, None, :]
    mixing = (jnp.where(causal, jnp.exp(jnp.where(causal, gap, 0.0)), 0.0) * scores).astype(
        jnp.bfloat16
    )
    intra = jnp.einsum("khls,kshp->klhp", mixing, inputs, preferred_element_type=jnp.float32)
    tail_decay = jnp.exp(cum_heads[:, :, -1:] - cum_heads)
    b_heads = jnp.repeat(b_grouped, per_group, axis=2)
    weighted_b = (
        b_heads.astype(jnp.float32) * jnp.transpose(tail_decay, (0, 2, 1))[..., None]
    ).astype(jnp.bfloat16)
    block_state = jnp.einsum(
        "klhn,klhp->khnp", weighted_b, inputs, preferred_element_type=jnp.float32
    )
    block_decay = cum_heads[:, :, -1]

    def advance(carried_state, pair):
        decay_here, state_here = pair
        return (jnp.exp(decay_here)[:, None, None] * carried_state + state_here, carried_state)

    zero_state = jnp.zeros((head_count, state_width, head_width), jnp.float32)
    device_state, local_starts = lax.scan(advance, zero_state, (block_decay, block_state))
    device_decay = jnp.sum(block_decay, axis=0)
    zero_decay = jnp.zeros((head_count,), jnp.float32)
    total_decay, incoming = prefix(
        (device_decay, device_state), "seq", carry_combine, (zero_decay, zero_state)
    )
    before_block = jnp.cumsum(block_decay, axis=0) - block_decay
    starts = local_starts + jnp.exp(before_block)[:, :, None, None] * incoming[None]
    c_heads = jnp.repeat(c_grouped, per_group, axis=2).astype(jnp.float32)
    carried = jnp.einsum("klhn,khnp->klhp", c_heads, starts, precision=lax.Precision.HIGHEST)
    carried = carried * jnp.exp(cum)[..., None]
    mixed = intra + carried + skip_d[None, None, :, None] * inputs.astype(jnp.float32)
    gated = mixed * jax.nn.silu(
        gate_z.reshape(block_count, SPAN, head_count, head_width).astype(jnp.float32)
    )
    grouped = gated.reshape(seq_rows, group_count, per_group * head_width)
    grouped = grouped * lax.rsqrt(jnp.mean(grouped * grouped, axis=-1, keepdims=True) + 1e-05)
    ssd_out = (grouped.reshape(seq_rows, channels) * norm_gain[None, :]).astype(jnp.bfloat16)
    partial_sum = jnp.dot(
        ssd_out,
        lax.all_gather(w_out, "seq", axis=1, tiled=True),
        preferred_element_type=jnp.float32,
    )
    mixer_out = lax.psum_scatter(
        partial_sum.astype(jnp.bfloat16), "head", scatter_dimension=0, tiled=True
    ).astype(jnp.float32)
    unit = refusal / jnp.sqrt(jnp.sum(refusal * refusal) + 1e-06)
    hidden = residual.astype(jnp.float32) + mixer_out
    coef = jnp.dot(hidden, unit, precision=lax.Precision.HIGHEST)
    stream = (hidden - coef[:, None] * unit[None, :]).astype(jnp.bfloat16)
    stream_float = stream.astype(jnp.float32)
    normed = (
        stream_float
        * lax.rsqrt(jnp.mean(stream_float * stream_float, axis=-1, keepdims=True) + 1e-05)
        * stream_gain[None, :]
    ).astype(jnp.bfloat16)
    all_rows = lax.all_gather(normed, "head", axis=0, tiled=True)
    next_float = jnp.dot(
        all_rows,
        lax.all_gather(w_in, "seq", axis=0, tiled=True),
        preferred_element_type=jnp.float32,
    )
    return (stream, next_float.astype(jnp.bfloat16))


def solution(mesh):
    in_specs = (
        P("seq", "head"),
        P("seq", "head"),
        P("seq", "head", None),
        P("seq", "head", None),
        P("seq", "head"),
        P("head"),
        P("head"),
        P("head", "seq"),
        P(("seq", "head"), None),
        P(),
        P(),
        P("seq", "head"),
    )
    out_specs = (P(("seq", "head"), None), P("seq", "head"))
    return jax.shard_map(body, mesh=mesh, in_specs=in_specs, out_specs=out_specs, check_vma=False)
```

profile of v0, /device:TPU:1, one launch (start us, length us, event | category | flops | bytes accessed | tf_op | source)
XLA Modules:
  0.0 529.7 jit_solution(17022700494069063450)
XLA Ops:
  10.4 4.0 reshape.182
  14.4 2.8 copy.50
  17.2 2.0 convert_element_type.84
  19.1 5.1 fusion.4
  24.2 6.9 %while.27 = (s32[]{:T(128)}, f32[16,256,64]{2,1,0:T(8,128)S(1)}, f32[2,16,256,64]{3,2,1,0:T(8,128)}, f32[2,16]{1,0:T(2,128)S(1)}, f32[2,16,256,64]{3,2,1,0:T(8,128)}, /*index=5*/s32[]{:T(128)}, s32[]{:T(128)}) while((s32[]{:T(128)}, f32[16,256,64]{2,1,0:T(8,128)S(1)}, f32[2,16,256,64]{3,2,1,0:T(8,128)}, f32[2,16]{1,0:T(2,128)S(1)}, ...), condition=%wide.region_3.4_spmd.clone, body=%wide.region_2.3_spmd.clone.sunk | while | flops 1048579 | bytes 14680892 | solution.py:92
  34.7 76.6 %all-reduce = bf16[512]{0:T(512)(128)(2,1)S(1)} all-reduce(bf16[512]{0:T(512)(128)(2,1)S(1)} %dynamic-update-slice), channel_id=2, replica_groups=mesh['seq'=32,'head'=8] {'seq'}, use_global_device_ids=true, to_apply=%add | all-reduce | flops 512 | bytes 2048
  111.4 2.0 fusion.27
  113.4 2.6 reshape.183
  116.0 4.6 copy.59
  120.6 25.5 %all-gather.13.cloned.1.call-done = bf16[512,256,64]{1,2,0:T(8,128)(2,1)} async-done(((bf16[16,256,64]{1,2,0:T(8,128)(2,1)}), bf16[512,256,64]{1,2,0:T(8,128)(2,1)}) %all-gather.13.cloned.1.call-update) | async-done | bytes 16777232 | tf_op jit(solution)/shard_map/all_gather | solution.py:12
  146.1 144.1 %while.28 = (s32[]{:T(128)}, f32[16,256,64]{2,1,0:T(8,128)S(1)}, s32[]{:T(128)}, bf16[32,16]{1,0:T(8,128)(2,1)S(1)}, bf16[32,16,256,64]{2,3,1,0:T(8,128)(2,1)}, /*index=5*/s32[]{:T(128)}, s32[]{:T(128)}) while((s32[]{:T(128)}, f32[16,256,64]{2,1,0:T(8,128)S(1)}, s32[]{:T(128)}, bf16[32,16]{1,0:T(8,128)(2,1)S(1)}, ...), condition=%wide.region_7.8_spmd.clone, body=%wide.region_6.7_spmd.clone.sunk | while | flops 1310740 | bytes 4718857 | solution.py:29
  150.6 1.9 constant_dynamic-slice_fusion.3
  159.6 1.9 constant_dynamic-slice_fusion.3
  164.1 1.9 constant_dynamic-slice_fusion.3
  168.5 1.9 constant_dynamic-slice_fusion.3
  173.1 1.9 constant_dynamic-slice_fusion.3
  177.6 1.9 constant_dynamic-slice_fusion.3
  182.1 1.9 constant_dynamic-slice_fusion.3
  186.6 1.9 constant_dynamic-slice_fusion.3
  191.1 1.9 constant_dynamic-slice_fusion.3
  195.5 1.9 constant_dynamic-slice_fusion.3
  200.1 1.9 constant_dynamic-slice_fusion.3
  213.5 1.9 constant_dynamic-slice_fusion.3
  227.0 2.0 constant_dynamic-slice_fusion.3
  290.3 6.0 %fusion.5 = f32[2,16,64,256]{3,2,1,0:T(8,128)S(1)} fusion(f32[2,16,256,64]{3,2,1,0:T(8,128)} %get-tuple-element.124, bf16[2,256,256]{2,1,0:T(8,128)(2,1)S(1)} %bitcast.79, f32[16,256,64]{2,1,0:T(8,128)S(1)} %get-tuple-element.126, f32[2,16]{1,0:T(2,128)S(1)} %subtract_exponential_fusion), kind=kOutput, calls=%fused_computation.14 | convolution fusion | flops 1611661312 | bytes 5505152 | tf_op jit(solution)/shard_map/klhn,khnp->klhp/dot_general | solution.py:101
  296.4 3.0 multiply_reduce_fusion
  302.6 10.9 %convolution_convert_fusion = bf16[512,4096]{1,0:T(8,128)(2,1)} fusion(bf16[1024,4096]{1,0:T(8,128)(2,1)} %all-gather.7.cloned.1.call-done, f32[512,1024]{0,1:T(8,128)} %bitcast.81, f32[1024]{0:T(1024)S(1)} %copy-done.13, f32[512]{0:T(512)S(1)} %bitcast.87), kind=kOutput, calls=%fused_computation.11 | convolution fusion | flops 4298637312 | bytes 14686208 | tf_op jit(solution)/shard_map/dot_general | solution.py:110
  315.6 61.8 %reduce-scatter.2.cloned.1.call-done = bf16[64,4096]{1,0:T(8,128)(2,1)} async-done(((bf16[512,4096]{1,0:T(8,128)(2,1)}), bf16[64,4096]{1,0:T(8,128)(2,1)}) %reduce-scatter.2.cloned.1.call-update) | async-done | bytes 524304 | tf_op jit(solution)/shard_map/reduce_scatter | solution.py:115
  377.4 2.0 convolution_bitcast_fusion
  381.8 73.2 %all-gather.11.cloned.1.call-done = bf16[4096,1024]{1,0:T(8,128)(2,1)} async-done(((bf16[128,1024]{1,0:T(8,128)(2,1)}), bf16[4096,1024]{1,0:T(8,128)(2,1)}) %all-gather.11.cloned.1.call-update) | async-done | bytes 8388624 | tf_op jit(solution)/shard_map/all_gather | solution.py:131
  455.0 57.9 %all-gather.9.cloned.1.call-done = bf16[512,4096]{1,0:T(8,128)(2,1)} async-done(((bf16[64,4096]{1,0:T(8,128)(2,1)}), bf16[512,4096]{1,0:T(8,128)(2,1)}) %all-gather.9.cloned.1.call-update) | async-done | bytes 4194320 | tf_op jit(solution)/shard_map/all_gather | solution.py:128
  513.0 10.1 %convolution_convert_fusion.1 = bf16[512,1024]{1,0:T(8,128)(2,1)} fusion(bf16[512,4096]{1,0:T(8,128)(2,1)} %all-gather.9.cloned.1.call-done, bf16[4096,1024]{1,0:T(8,128)(2,1)} %all-gather.11.cloned.1.call-done), kind=kOutput, calls=%fused_computation.33 | convolution fusion | flops 4295491584 | bytes 13631488 | tf_op jit(solution)/shard_map/dot_general | solution.py:129
  (194 shorter events, 137.8 us)
Async XLA Ops:
  7.2 104.2 %copy-start = (bf16[512,1,256]{2,0,1:T(8,128)(2,1)S(1)}, bf16[512,1,256]{2,0,1:T(8,128)(2,1)}, u32[]{:S(2)}) copy-start(bf16[512,1,256]{2,0,1:T(8,128)(2,1)} %param.19) | copy-start | bytes 786436
  7.2 138.9 %all-gather.13.cloned.1.call-start = ((), (), s32[]{:S(2)}) async-start(), calls=%async_computation.5 | async-start | bytes 17301504 | tf_op jit(solution)/shard_map/all_gather | solution.py:12
  17.2 7.1 %copy-start.3 = (bf16[2,256,16,64]{1,3,2,0:T(8,128)(2,1)}, bf16[2,256,16,64]{1,3,2,0:T(8,128)(2,1)S(1)}, u32[]{:S(2)}) copy-start(bf16[2,256,16,64]{1,3,2,0:T(8,128)(2,1)S(1)} %copy.50) | copy-start | bytes 3145732
  24.2 2.9 copy-start.2
  27.7 2.9 copy-start.2
  31.2 2.1 copy-start.15
  31.2 82.2 %copy-start.8 = (bf16[512,1024]{1,0:T(8,128)(2,1)S(1)}, bf16[512,1024]{1,0:T(8,128)(2,1)}, u32[]{:S(2)}) copy-start(bf16[512,1024]{1,0:T(8,128)(2,1)} %param.17) | copy-start | bytes 3145732
  32.3 270.3 %all-gather.7.cloned.1.call-start = ((), (), s32[]{:S(2)}) async-start(), calls=%async_computation.1 | async-start | bytes 8650752 | tf_op jit(solution)/shard_map/all_gather | solution.py:112
  33.1 344.3 %reduce-scatter.2.cloned.1.call-start = ((), (), s32[]{:S(2)}) async-start(), calls=%async_computation.2 | async-start | bytes 4718592 | tf_op jit(solution)/shard_map/reduce_scatter | solution.py:115
  290.2 6.1 %copy-start.4 = (bf16[2,256,16,64]{1,3,2,0:T(8,128)(2,1)S(1)}, bf16[2,256,16,64]{1,3,2,0:T(8,128)(2,1)}, u32[]{:S(2)}) copy-start(bf16[2,256,16,64]{1,3,2,0:T(8,128)(2,1)} %copy-done.3) | copy-start | bytes 3145732
  290.2 6.1 %copy-start.5 = (f32[2,256,16,64]{1,3,2,0:T(8,128)S(1)}, f32[2,256,16,64]{1,3,2,0:T(8,128)}, u32[]{:S(2)}) copy-start(f32[2,256,16,64]{1,3,2,0:T(8,128)} %copy.59) | copy-start | bytes 6291460
  290.2 6.1 %copy-start.9 = (f32[2,256,256]{2,1,0:T(8,128)S(1)}, f32[2,256,256]{2,1,0:T(8,128)}, u32[]{:S(2)}) copy-start(f32[2,256,256]{2,1,0:T(8,128)} %fusion.27) | copy-start | bytes 1572868
  290.2 6.1 %copy-start.11 = (f32[2,256,16]{1,2,0:T(8,128)S(1)}, f32[2,256,16]{1,2,0:T(8,128)}, u32[]{:S(2)}) copy-start(f32[2,256,16]{1,2,0:T(8,128)} %get-tuple-element.212) | copy-start | bytes 98308
  290.3 6.1 %copy-start.14 = (f32[16]{0:T(128)S(1)}, f32[16]{0:T(128)}, u32[]{:S(2)}) copy-start(f32[16]{0:T(128)} %param.21) | copy-start | bytes 196
  301.1 1.6 copy-start.13
  313.5 0.7 copy-start.10
  313.5 63.8 %copy-start.6 = (bf16[64,4096]{1,0:T(8,128)(2,1)S(1)}, bf16[64,4096]{1,0:T(8,128)(2,1)}, u32[]{:S(2)}) copy-start(bf16[64,4096]{1,0:T(8,128)(2,1)} %param.24) | copy-start | bytes 1572868
  313.6 67.2 %copy-start.12 = (f32[4096]{0:T(1024)S(1)}, f32[4096]{0:T(1024)}, u32[]{:S(2)}) copy-start(f32[4096]{0:T(1024)} %param.26) | copy-start | bytes 49156
  313.6 141.4 %all-gather.11.cloned.1.call-start = ((), (), s32[]{:S(2)}) async-start(), calls=%async_computation.4 | async-start | bytes 8650752 | tf_op jit(solution)/shard_map/all_gather | solution.py:131
  314.2 198.8 %all-gather.9.cloned.1.call-start = ((), (), s32[]{:S(2)}) async-start(), calls=%async_computation.3 | async-start | bytes 4718592 | tf_op jit(solution)/shard_map/all_gather | solution.py:128
  380.8 142.3 %copy-start.7 = (bf16[64,4096]{1,0:T(8,128)(2,1)}, bf16[64,4096]{1,0:T(8,128)(2,1)S(1)}, u32[]{:S(2)}) copy-start(bf16[64,4096]{1,0:T(8,128)(2,1)S(1)} %get-tuple-element.211) | copy-start | bytes 1572868
  513.0 10.2 %copy-start.1 = (bf16[512,1,256]{2,0,1:T(8,128)(2,1)S(1)}, bf16[512,1,256]{2,0,1:T(8,128)(2,1)}, u32[]{:S(2)}) copy-start(bf16[512,1,256]{2,0,1:T(8,128)(2,1)} %param.19) | copy-start | bytes 786436
Sparse Core Ops, SparseCore 0:
  32.5 113.5 all-gather.12
  148.6 93.9 all-gather.6
  313.7 63.6 reduce-scatter.1
  379.8 75.2 all-gather.10
  457.2 55.6 all-gather.8
where the time goes:
time: 533 us; the launch traced here: 530 us
  waiting for transfers between devices  220 us (41%)
  local copies, waits for them, and re-layouts  132 us (25%)
  blocking collectives  76.6 us (14%)
  other arithmetic  44.8 us (8%)
  matrix products  39.3 us (7%)
  between operations  15.4 us (3%)
    dynamic_slice x64, local copies, waits for them, and re-layouts, turn(): part[k].astype(own.dtype)  109 us
    unnamed x1, blocking collectives  76.6 us
    all_gather x1, waiting for transfers between devices, body(): lax.all_gather(w_in, 'seq', axis=0, tiled=True)  73.2 us
    reduce_scatter x1, waiting for transfers between devices, body(): lax.psum_scatter(partial_sum.astype(jnp.bfloat16), 'head', scatter_dimens...  61.8 us
    all_gather x1, waiting for transfers between devices, body(): all_rows = lax.all_gather(normed, 'head', axis=0, tiled=True)  57.9 us
    select_n x32, other arithmetic, turn(): return jax.tree.map(lambda a, b: jnp.where(reached, a, b), new, before)  33 us
    all_gather x1, waiting for transfers between devices, prefix(): lax.all_gather(part.astype(kind), axis)  25.5 us
    dot_general x1, matrix products, body(): jnp.dot(ssd_out, lax.all_gather(w_out, 'seq', axis=1, tiled=True), prefer...  10.9 us
  transfers between devices with their start and end apart: 5, of which 4 were waited for; matrix products, arithmetic and copies ran while one was open for 32% of the time, Pallas kernels for 0%

commit v1 on v0

--- a/solution.py
+++ b/solution.py
@@ -128,7 +128,9 @@
     all_rows = lax.all_gather(normed, "head", axis=0, tiled=True)
     next_float = jnp.dot(
         all_rows,
-        lax.all_gather(w_in, "seq", axis=0, tiled=True),
+        jnp.concatenate(
+            lax.all_to_all(jnp.stack([w_in] * lax.axis_size("seq")), "seq", 0, 0), axis=0
+        ),
         preferred_element_type=jnp.float32,
     )
     return (stream, next_float.astype(jnp.bfloat16))

time: 533 us -> 617 us (1.16)
  waiting for transfers between devices: 220 us -> 281 us
  starting transfers between devices: 0.2 us -> 19.5 us
    all_to_all x0 -> x1, waiting for transfers between devices: none -> 120 us  [body(): lax.all_to_all(jnp.stack([w_in] * lax.axis_size('seq')), 'seq', 0, 0)]
    reduce_scatter x1, waiting for transfers between devices: 61.8 us -> 137 us  [body(): lax.psum_scatter(partial_sum.astype(jnp.bfloat16), 'head', scatter_dimens...]
    all_gather x1 -> x0, waiting for transfers between devices: 73.2 us -> none  [body(): lax.all_gather(w_in, 'seq', axis=0, tiled=True)]
    all_gather x1, waiting for transfers between devices: 57.9 us -> 0.01 us  [body(): all_rows = lax.all_gather(normed, 'head', axis=0, tiled=True)]
    all_to_all x0 -> x1, starting transfers between devices: none -> 19.3 us  [body(): lax.all_to_all(jnp.stack([w_in] * lax.axis_size('seq')), 'seq', 0, 0)]
  transfers between devices with their start and end apart: 5 -> 5, of which waited for: 4 -> 3; matrix products, arithmetic and copies ran while one was open for 32% -> 28% of each run, Pallas kernels for 0% -> 0%
where the time goes in v1:
time: 617 us; the launch traced here: 613 us
  waiting for transfers between devices  281 us (46%)
  local copies, waits for them, and re-layouts  136 us (22%)
  blocking collectives  76.5 us (12%)
  other arithmetic  44.7 us (7%)
  matrix products  38 us (6%)
  starting transfers between devices  19.5 us (3%)
  between operations  15.4 us (2%)
    reduce_scatter x1, waiting for transfers between devices, body(): lax.psum_scatter(partial_sum.astype(jnp.bfloat16), 'head', scatter_dimens...  137 us
    all_to_all x1, waiting for transfers between devices, body(): lax.all_to_all(jnp.stack([w_in] * lax.axis_size('seq')), 'seq', 0, 0)  120 us
    dynamic_slice x64, local copies, waits for them, and re-layouts, turn(): part[k].astype(own.dtype)  109 us
    unnamed x1, blocking collectives  76.5 us
    select_n x32, other arithmetic, turn(): return jax.tree.map(lambda a, b: jnp.where(reached, a, b), new, before)  33 us
    all_gather x1, waiting for transfers between devices, prefix(): lax.all_gather(part.astype(kind), axis)  23.4 us
    all_to_all x1, starting transfers between devices, body(): lax.all_to_all(jnp.stack([w_in] * lax.axis_size('seq')), 'seq', 0, 0)  19.3 us
  transfers between devices with their start and end apart: 5, of which 3 were waited for; matrix products, arithmetic and copies ran while one was open for 28% of the time, Pallas kernels for 0%

profile of v1, /device:TPU:1, one launch (start us, length us, event | category | flops | bytes accessed | tf_op | source)
XLA Modules:
  0.0 612.7 jit_solution(16178177677445454261)
XLA Ops:
  10.4 4.0 reshape.188
  14.4 2.8 copy.50
  17.2 2.0 convert_element_type.84
  19.1 5.1 fusion.4
  24.2 6.9 %while.27 = (s32[]{:T(128)}, f32[16,256,64]{2,1,0:T(8,128)S(1)}, f32[2,16,256,64]{3,2,1,0:T(8,128)}, f32[2,16]{1,0:T(2,128)S(1)}, f32[2,16,256,64]{3,2,1,0:T(8,128)}, /*index=5*/s32[]{:T(128)}, s32[]{:T(128)}) while((s32[]{:T(128)}, f32[16,256,64]{2,1,0:T(8,128)S(1)}, f32[2,16,256,64]{3,2,1,0:T(8,128)}, f32[2,16]{1,0:T(2,128)S(1)}, ...), condition=%wide.region_3.4_spmd.clone, body=%wide.region_2.3_spmd.clone.sunk | while | flops 1048579 | bytes 14680892 | solution.py:92
  34.7 76.5 %all-reduce = bf16[512]{0:T(512)(128)(2,1)S(1)} all-reduce(bf16[512]{0:T(512)(128)(2,1)S(1)} %dynamic-update-slice), channel_id=2, replica_groups=mesh['seq'=32,'head'=8] {'seq'}, use_global_device_ids=true, to_apply=%add | all-reduce | flops 512 | bytes 2048
  111.4 2.0 fusion.27
  113.4 2.6 reshape.189
  116.0 4.6 copy.59
  120.6 23.4 %all-gather.10.cloned.1.call-done = bf16[512,256,64]{1,2,0:T(8,128)(2,1)} async-done(((bf16[16,256,64]{1,2,0:T(8,128)(2,1)}), bf16[512,256,64]{1,2,0:T(8,128)(2,1)}) %all-gather.10.cloned.1.call-update) | async-done | bytes 16777232 | tf_op jit(solution)/shard_map/all_gather | solution.py:12
  143.9 143.8 %while.28 = (s32[]{:T(128)}, f32[16,256,64]{2,1,0:T(8,128)S(1)}, s32[]{:T(128)}, bf16[32,16]{1,0:T(8,128)(2,1)S(1)}, bf16[32,16,256,64]{2,3,1,0:T(8,128)(2,1)}, /*index=5*/s32[]{:T(128)}, s32[]{:T(128)}) while((s32[]{:T(128)}, f32[16,256,64]{2,1,0:T(8,128)S(1)}, s32[]{:T(128)}, bf16[32,16]{1,0:T(8,128)(2,1)S(1)}, ...), condition=%wide.region_7.8_spmd.clone, body=%wide.region_6.7_spmd.clone.sunk | while | flops 1310740 | bytes 4718857 | solution.py:29
  148.4 1.9 constant_dynamic-slice_fusion.3
  152.9 1.9 constant_dynamic-slice_fusion.3
  157.4 1.9 constant_dynamic-slice_fusion.3
  161.9 1.9 constant_dynamic-slice_fusion.3
  166.4 1.9 constant_dynamic-slice_fusion.3
  170.9 1.9 constant_dynamic-slice_fusion.3
  175.4 1.9 constant_dynamic-slice_fusion.3
  184.4 1.9 constant_dynamic-slice_fusion.3
  188.9 1.9 constant_dynamic-slice_fusion.3
  197.8 1.9 constant_dynamic-slice_fusion.3
  211.3 1.9 constant_dynamic-slice_fusion.3
  229.3 1.9 constant_dynamic-slice_fusion.3
  287.8 6.0 fusion.5
  293.9 3.0 multiply_reduce_fusion
  299.3 9.7 %convolution_convert_fusion = bf16[512,4096]{1,0:T(8,128)(2,1)} fusion(bf16[1024,4096]{1,0:T(8,128)(2,1)} %all-gather.6.cloned.1.call-done, f32[512,1024]{0,1:T(8,128)S(1)} %bitcast.82, f32[1024]{0:T(1024)S(1)} %copy-done.14, f32[512]{0:T(512)S(1)} %bitcast.88), kind=kOutput, calls=%fused_computation.11 | convolution fusion | flops 4298637312 | bytes 14686208 | tf_op jit(solution)/shard_map/dot_general | solution.py:110
  309.9 4.3 stack.2
  314.2 19.3 %all-to-all-start = ((bf16[32,128,1024]{2,1,0:T(8,128)(2,1)}), bf16[32,128,1024]{2,1,0:T(8,128)(2,1)}, u32[]{:S(2)}, u32[]{:S(2)}) async-start(bf16[32,128,1024]{2,1,0:T(8,128)(2,1)} %stack.2), calls=%async_computation.1 | async-start | bytes 16777216 | tf_op jit(solution)/shard_map/all_to_all | solution.py:132
  334.9 137.1 %reduce-scatter.2.cloned.1.call-done = bf16[64,4096]{1,0:T(8,128)(2,1)} async-done(((bf16[512,4096]{1,0:T(8,128)(2,1)}), bf16[64,4096]{1,0:T(8,128)(2,1)}) %reduce-scatter.2.cloned.1.call-update) | async-done | bytes 524304 | tf_op jit(solution)/shard_map/reduce_scatter | solution.py:115
  472.0 2.0 convolution_bitcast_fusion
  476.4 119.5 %all-to-all-done = bf16[32,128,1024]{2,1,0:T(8,128)(2,1)} async-done(((bf16[32,128,1024]{2,1,0:T(8,128)(2,1)}), bf16[32,128,1024]{2,1,0:T(8,128)(2,1)}, u32[]{:S(2)}, u32[]{:S(2)}) %all-to-all-start) | async-done | bytes 8388640 | tf_op jit(solution)/shard_map/all_to_all | solution.py:132
  596.0 10.2 %convolution_convert_fusion.1 = bf16[512,1024]{1,0:T(8,128)(2,1)} fusion(bf16[512,4096]{1,0:T(8,128)(2,1)} %all-gather.8.cloned.1.call-done, bf16[4096,1024]{1,0:T(8,128)(2,1)} %bitcast.11), kind=kOutput, calls=%fused_computation.33 | convolution fusion | flops 4295491584 | bytes 13631488 | tf_op jit(solution)/shard_map/dot_general | solution.py:129
  (196 shorter events, 139.2 us)
Async XLA Ops:
  7.2 104.2 %copy-start = (bf16[512,1,256]{2,0,1:T(8,128)(2,1)S(1)}, bf16[512,1,256]{2,0,1:T(8,128)(2,1)}, u32[]{:S(2)}) copy-start(bf16[512,1,256]{2,0,1:T(8,128)(2,1)} %param.19) | copy-start | bytes 786436
  7.2 136.8 %all-gather.10.cloned.1.call-start = ((), (), s32[]{:S(2)}) async-start(), calls=%async_computation.5 | async-start | bytes 17301504 | tf_op jit(solution)/shard_map/all_gather | solution.py:12
  17.2 7.1 %copy-start.3 = (bf16[2,256,16,64]{1,3,2,0:T(8,128)(2,1)}, bf16[2,256,16,64]{1,3,2,0:T(8,128)(2,1)S(1)}, u32[]{:S(2)}) copy-start(bf16[2,256,16,64]{1,3,2,0:T(8,128)(2,1)S(1)} %copy.50) | copy-start | bytes 3145732
  24.2 2.9 copy-start.2
  27.7 2.9 copy-start.2
  31.2 2.1 copy-start.16
  31.2 82.2 %copy-start.8 = (bf16[512,1024]{1,0:T(8,128)(2,1)S(1)}, bf16[512,1024]{1,0:T(8,128)(2,1)}, u32[]{:S(2)}) copy-start(bf16[512,1024]{1,0:T(8,128)(2,1)} %param.17) | copy-start | bytes 3145732
  32.3 266.5 %all-gather.6.cloned.1.call-start = ((), (), s32[]{:S(2)}) async-start(), calls=%async_computation.2 | async-start | bytes 8650752 | tf_op jit(solution)/shard_map/all_gather | solution.py:112
  33.1 438.9 %reduce-scatter.2.cloned.1.call-start = ((), (), s32[]{:S(2)}) async-start(), calls=%async_computation.3 | async-start | bytes 4718592 | tf_op jit(solution)/shard_map/reduce_scatter | solution.py:115
  287.7 6.1 copy-start.4
  287.7 6.1 copy-start.5
  287.8 6.1 copy-start.9
  287.8 6.1 copy-start.12
  287.8 6.1 copy-start.15
  298.6 0.7 copy-start.14
  308.9 0.9 copy-start.10
  314.2 19.4 %copy-start.11 = (f32[4096]{0:T(1024)S(1)}, f32[4096]{0:T(1024)}, u32[]{:S(2)}) copy-start(f32[4096]{0:T(1024)} %param.25) | copy-start | bytes 49156
  314.2 157.8 %copy-start.6 = (bf16[64,4096]{1,0:T(8,128)(2,1)S(1)}, bf16[64,4096]{1,0:T(8,128)(2,1)}, u32[]{:S(2)}) copy-start(bf16[64,4096]{1,0:T(8,128)(2,1)} %param.24) | copy-start | bytes 1572868
  314.2 281.8 %all-to-all-start = ((bf16[32,128,1024]{2,1,0:T(8,128)(2,1)}), bf16[32,128,1024]{2,1,0:T(8,128)(2,1)}, u32[]{:S(2)}, u32[]{:S(2)}) async-start(bf16[32,128,1024]{2,1,0:T(8,128)(2,1)} %stack.2), calls=%async_computation.1 | async-start | bytes 16777216 | tf_op jit(solution)/shard_map/all_to_all | solution.py:132
  333.5 141.9 %copy-start.13 = (f32[4096]{0:T(1024)S(1)}, f32[4096]{0:T(1024)}, u32[]{:S(2)}) copy-start(f32[4096]{0:T(1024)} %param.26) | copy-start | bytes 49156
  333.5 262.4 %all-gather.8.cloned.1.call-start = ((), (), s32[]{:S(2)}) async-start(), calls=%async_computation.4 | async-start | bytes 4718592 | tf_op jit(solution)/shard_map/all_gather | solution.py:128
  475.4 130.7 %copy-start.7 = (bf16[64,4096]{1,0:T(8,128)(2,1)}, bf16[64,4096]{1,0:T(8,128)(2,1)S(1)}, u32[]{:S(2)}) copy-start(bf16[64,4096]{1,0:T(8,128)(2,1)S(1)} %get-tuple-element.211) | copy-start | bytes 1572868
  596.0 10.2 %copy-start.1 = (bf16[512,1,256]{2,0,1:T(8,128)(2,1)S(1)}, bf16[512,1,256]{2,0,1:T(8,128)(2,1)}, u32[]{:S(2)}) copy-start(bf16[512,1,256]{2,0,1:T(8,128)(2,1)} %param.19) | copy-start | bytes 786436
Sparse Core Ops, SparseCore 0:
  32.5 111.4 all-gather.9
  146.4 96.5 all-gather.5
  309.1 162.8 reduce-scatter.1
  476.6 117.5 all-gather.7
